TPU v7x, 512 devices: a whole 4x4x16 slice. The times are simulated.
512 devices in a mesh: patch: 128 (over z, y, core), mp: 4 (over x).
Axes of the slice: x: 4, y: 4, z: 16, core: 2. Of those that a mesh axis runs over, the one named last changes fastest.
Arguments:
- features: bfloat16 [65536, 1024], P('patch'), may hold values from -16 to 16
- gain_attn: float32 [1024], replicated, may hold values from 0.1 to 1.9
- w_qkv: bfloat16 [3, 1024, 1024], P(None, None, 'mp'), as said below
- w_out: bfloat16 [1024, 1024], P('mp'), may hold values from -0.1875 to 0.1875
- gain_mlp: float32 [1024], replicated, may hold values from 0.1 to 1.9
- w_up: bfloat16 [1024, 2048], P(None, 'mp'), may hold values from -0.1875 to 0.1875
- w_down: bfloat16 [2048, 1024], P('mp'), may hold values from -0.125 to 0.125
- neighbours: int32 [512, 8], replicated, may hold values from 0 to 511, as said below
Outputs:
- layer_out: bfloat16 [65536, 1024], P('patch', 'mp')
Inputs may be any that keep to these rules, and one draw needn't show every extreme that they name: `neighbours`: row p lists 8 different patches; the first is p itself. Patch q belongs to device q // 4 of the patch axis, and every listed patch belongs to a device whose index differs from that of p's device by at most 2 around the patch axis (the lining closes into a cycle). `w_qkv`: projection weights of mean zero.
All inputs are finite; a program needn't handle non-finite values.
Results may differ from a plain program's by a relative error of at most 0.012.
Values may be sent and summed in bfloat16 or wider, within the bound.
No kernel may reach another device: no remote copies, remote signals or barrier semaphores. Data moves between devices by JAX's collectives and lax.ppermute only.
A program may use at most 64 MiB of HBM per device.

v0:
```python
import jax
import jax.numpy as jnp
from jax import lax
from jax.sharding import PartitionSpec as P

D = 1024
HD = 64
PN = 128
K_NB = 8
REACH = 2


def from_behind(array, axis, by):
    length = lax.axis_size(axis)
    return lax.ppermute(array, axis, [(i, (i + by) % length) for i in range(length)])


def normalize(rows, gain):
    rows32 = rows.astype(jnp.float32)
    mean_sq = jnp.mean(rows32 * rows32, axis=-1, keepdims=True)
    return (rows32 * lax.rsqrt(mean_sq + 1e-05) * gain).astype(jnp.bfloat16)


def per_device(features, gain_attn, w_qkv, w_out, gain_mlp, w_up, w_down, neighbours):
    row_count = features.shape[0]
    patches_here = row_count // PN
    heads_here = w_qkv.shape[2] // HD
    normed = normalize(features, gain_attn)
    queries = jnp.dot(normed, w_qkv[0], preferred_element_type=jnp.float32).astype(jnp.bfloat16)
    own_keys = (
        jnp.dot(normed, w_qkv[1], preferred_element_type=jnp.float32)
        .astype(jnp.bfloat16)
        .reshape(patches_here, PN, -1)
    )
    own_vals = (
        jnp.dot(normed, w_qkv[2], preferred_element_type=jnp.float32)
        .astype(jnp.bfloat16)
        .reshape(patches_here, PN, -1)
    )
    window = {0: (own_keys, own_vals)}
    for offset in range(-REACH, REACH + 1):
        if offset != 0:
            window[offset] = from_behind((own_keys, own_vals), "patch", -offset)
    keys_win = jnp.concatenate([window[offset][0] for offset in range(-REACH, REACH + 1)], axis=0)
    vals_win = jnp.concatenate([window[offset][1] for offset in range(-REACH, REACH + 1)], axis=0)
    device = lax.axis_index("patch")
    n_dev = lax.axis_size("patch")
    listed = lax.dynamic_slice_in_dim(neighbours, device * patches_here, patches_here, 0)
    owner_dev = listed // patches_here
    offset_dev = jnp.mod(owner_dev - device + n_dev // 2, n_dev) - n_dev // 2
    slot_index = (offset_dev + REACH) * patches_here + jnp.mod(listed, patches_here)
    keys_nb = keys_win[slot_index].reshape(patches_here, K_NB * PN, heads_here, HD)
    vals_nb = vals_win[slot_index].reshape(patches_here, K_NB * PN, heads_here, HD)
    query_blk = queries.reshape(patches_here, PN, heads_here, HD)
    scores = jnp.einsum(
        "pqhd,pkhd->phqk", query_blk, keys_nb, preferred_element_type=jnp.float32
    ) * (1.0 / HD**0.5)
    probs = jax.nn.softmax(scores, axis=-1).astype(jnp.bfloat16)
    mixed_rows = jnp.einsum("phqk,pkhd->pqhd", probs, vals_nb, preferred_element_type=jnp.float32)
    attended = mixed_rows.astype(jnp.bfloat16).reshape(row_count, heads_here * HD)
    partial_value = jnp.dot(attended, w_out, preferred_element_type=jnp.float32)
    col_share = lax.psum_scatter(
        partial_value.astype(jnp.bfloat16), "mp", scatter_dimension=1, tiled=True
    ).astype(jnp.float32)
    col_width = col_share.shape[1]
    col_begin = lax.axis_index("mp") * col_width
    residual_cols = (
        lax.dynamic_slice_in_dim(features, col_begin, col_width, 1).astype(jnp.float32) + col_share
    )
    gain_cols = lax.dynamic_slice_in_dim(gain_mlp, col_begin, col_width, 0)
    square_sum = lax.psum(jnp.sum(residual_cols * residual_cols, axis=1), "mp")
    inverse_rms = lax.rsqrt(square_sum / D + 1e-05)
    normed_cols = (residual_cols * inverse_rms[:, None] * gain_cols).astype(jnp.bfloat16)
    normed2 = lax.all_gather(normed_cols, "mp", axis=1, tiled=True)
    hidden = jax.nn.gelu(
        jnp.dot(normed2, w_up, preferred_element_type=jnp.float32), approximate=True
    ).astype(jnp.bfloat16)
    down_term = jnp.dot(hidden, w_down, preferred_element_type=jnp.float32)
    down_cols = lax.psum_scatter(
        down_term.astype(jnp.bfloat16), "mp", scatter_dimension=1, tiled=True
    ).astype(jnp.float32)
    return (residual_cols + down_cols).astype(jnp.bfloat16)


def solution(mesh):
    return jax.shard_map(
        per_device,
        mesh=mesh,
        in_specs=(
            P("patch", None),
            P(),
            P(None, None, "mp"),
            P("mp", None),
            P(),
            P(None, "mp"),
            P("mp", None),
            P(),
        ),
        out_specs=P("patch", "mp"),
        check_vma=False,
    )
```

profile of v0, /device:TPU:8, one launch (start us, length us, event | category | flops | bytes accessed | tf_op | source)
XLA Modules:
  0.0 209.8 jit_solution(8594160232992480794)
XLA Ops:
  6.5 0.0 copy-start.6
  6.6 1.7 fusion.9
  8.2 1.9 convolution_convert_fusion.2
  10.1 3.5 %collective-permute-start.4 = (bf16[4,128,256]{2,1,0:T(8,128)(2,1)S(1)}, bf16[4,128,256]{2,1,0:T(8,128)(2,1)}, u32[]{:S(2)}, u32[]{:S(2)}) collective-permute-start(bf16[4,128,256]{2,1,0:T(8,128)(2,1)S(1)} %bitcast.30), channel_id=1, source_target_pairs={{0,8},{4,12},{8,16},{12,20},{16,24},{20,28},{24,32},{28,36},{32,40... | collective-permute-start | bytes 786440 | tf_op jit(solution)/shard_map/ppermute | solution.py:15
  13.6 1.9 collective-permute-start.5
  15.5 3.6 %collective-permute-start.6 = (bf16[4,128,256]{2,1,0:T(8,128)(2,1)S(1)}, bf16[4,128,256]{2,1,0:T(8,128)(2,1)S(1)}, u32[]{:S(2)}, u32[]{:S(2)}) collective-permute-start(bf16[4,128,256]{2,1,0:T(8,128)(2,1)S(1)} %bitcast.32), channel_id=1, source_target_pairs={{0,508},{4,0},{8,4},{12,8},{16,12},{20,16},{24,20},{28,24},{32,28}... | collective-permute-start | bytes 786440 | tf_op jit(solution)/shard_map/ppermute | solution.py:15
  19.2 10.4 %collective-permute-start.7 = (bf16[4,128,256]{2,1,0:T(8,128)(2,1)S(1)}, bf16[4,128,256]{2,1,0:T(8,128)(2,1)S(1)}, u32[]{:S(2)}, u32[]{:S(2)}) collective-permute-start(bf16[4,128,256]{2,1,0:T(8,128)(2,1)S(1)} %bitcast.33), channel_id=1, source_target_pairs={{0,504},{4,508},{8,0},{12,4},{16,8},{20,12},{24,16},{28,20},{32,24... | collective-permute-start | bytes 786440 | tf_op jit(solution)/shard_map/ppermute | solution.py:15
  29.6 0.0 copy-done.2
  29.6 0.0 copy-done.8
  29.6 0.0 copy-done.6
  29.7 0.5 convolution_convert_fusion.4
  30.1 1.9 collective-permute-start
  32.1 0.5 convolution_convert_fusion.3
  32.6 0.8 compare_select_fusion
  33.4 0.1 copy.17
  33.5 0.1 reshape.39
  33.5 1.0 reshape.60
  34.6 0.0 collective-permute-done.4
  34.6 1.9 collective-permute-start.1
  36.5 1.7 constant_dynamic-update-slice_fusion.9
  38.2 0.0 collective-permute-done.5
  38.2 3.6 %collective-permute-start.2 = (bf16[4,128,256]{2,1,0:T(8,128)(2,1)S(1)}, bf16[4,128,256]{2,1,0:T(8,128)(2,1)}, u32[]{:S(2)}, u32[]{:S(2)}) collective-permute-start(bf16[4,128,256]{2,1,0:T(8,128)(2,1)S(1)} %bitcast.27), channel_id=1, source_target_pairs={{0,508},{4,0},{8,4},{12,8},{16,12},{20,16},{24,20},{28,24},{32,28}... | collective-permute-start | bytes 786440 | tf_op jit(solution)/shard_map/ppermute | solution.py:15
  41.8 1.7 constant_dynamic-update-slice_fusion.8
  43.5 0.7 constant_dynamic-update-slice_fusion.7
  44.2 0.0 collective-permute-done.6
  44.2 7.5 %collective-permute-start.3 = (bf16[4,128,256]{2,1,0:T(8,128)(2,1)S(1)}, bf16[4,128,256]{2,1,0:T(8,128)(2,1)}, u32[]{:S(2)}, u32[]{:S(2)}) collective-permute-start(bf16[4,128,256]{2,1,0:T(8,128)(2,1)S(1)} %bitcast.28), channel_id=1, source_target_pairs={{0,504},{4,508},{8,0},{12,4},{16,8},{20,12},{24,16},{28,20},{32,24... | collective-permute-start | bytes 786440 | tf_op jit(solution)/shard_map/ppermute | solution.py:15
  51.7 0.7 constant_dynamic-update-slice_fusion.6
  52.4 0.0 collective-permute-done.7
  52.5 0.7 constant_dynamic-update-slice_fusion.5
  53.2 2.0 gather_fusion.1
  55.2 3.2 %reshape.61 = bf16[4,1024,4,64]{3,2,1,0:T(4,128)(2,1)} reshape(bf16[32,128,256]{2,1,0:T(8,128)(2,1)S(1)} %gather_fusion.1) | data formatting | bytes 4194304 | tf_op jit(solution)/shard_map/reshape | solution.py:52
  58.4 3.6 %fusion.4 = f32[4,4,128,1024]{3,2,1,0:T(8,128)S(1)} fusion(bf16[4,1024,4,64]{3,2,1,0:T(4,128)(2,1)} %reshape.61, bf16[4,128,4,64]{3,2,1,0:T(4,128)(2,1)} %reshape.60), kind=kOutput, calls=%fused_computation.7 | convolution fusion | flops 268435456 | bytes 10747904 | tf_op jit(solution)/shard_map/pqhd,pkhd->phqk/dot_general | solution.py:55
  62.1 2.2 %fusion.62 = f32[4,4,128]{2,1,0:T(4,128)S(1)} fusion(f32[4,4,128,1024]{3,2,1,0:T(8,128)S(1)} %fusion.4), kind=kOutput, calls=%fused_computation.87 | output fusion | flops 8389631 | bytes 8396800 | tf_op jit(solution)/shard_map/sub | solution.py:58
  64.2 1.0 copy-done.1
  65.3 0.0 collective-permute-done
  65.3 1.7 constant_dynamic-update-slice_fusion.4
  67.0 0.0 collective-permute-done.1
  67.0 1.7 constant_dynamic-update-slice_fusion.3
  68.6 0.7 constant_dynamic-update-slice_fusion.2
  69.4 0.0 collective-permute-done.2
  69.4 1.7 constant_dynamic-update-slice_fusion.1
  71.1 0.0 collective-permute-done.3
  71.1 1.7 constant_dynamic-update-slice_fusion
  72.7 2.0 gather_fusion
  74.7 3.3 %reshape.59 = bf16[4,1024,4,64]{3,2,1,0:T(4,128)(2,1)} reshape(bf16[32,128,256]{2,1,0:T(8,128)(2,1)S(1)} %gather_fusion) | data formatting | bytes 4194304 | tf_op jit(solution)/shard_map/reshape | solution.py:53
  78.0 12.1 %fusion.15 = bf16[4,128,4,64]{1,3,2,0:T(8,128)(2,1)S(1)} fusion(f32[4,4,128]{2,1,0:T(4,128)S(1)} %fusion.62, bf16[4,1024,4,64]{3,2,1,0:T(4,128)(2,1)} %reshape.59, f32[4,4,128,1024]{3,2,1,0:T(8,128)} %copy-done.1), kind=kOutput, calls=%fused_computation.24 | convolution fusion | flops 279055360 | bytes 10756096 | tf_op jit(solution)/shard_map/phqk,pkhd->pqhd/dot_general | solution.py:59
  90.1 0.0 copy-start.3
  90.2 0.2 copy.24
  90.4 1.4 convolution_convert_fusion
  91.8 0.0 reduce-scatter.3.cloned.1.call-update
  91.8 0.0 all-gather.2.cloned.1.call-start
  91.9 0.8 dynamic_slice.11
  92.7 28.3 %reduce-scatter.3.cloned.1.call-done = bf16[512,256]{1,0:T(8,128)(2,1)} async-done(((bf16[512,1024]{1,0:T(8,128)(2,1)}), bf16[512,256]{1,0:T(8,128)(2,1)}) %reduce-scatter.3.cloned.1.call-update) | async-done | bytes 262160 | tf_op jit(solution)/shard_map/reduce_scatter | solution.py:62
  121.1 1.1 multiply_reduce_fusion.1
  122.2 8.4 %psum.7 = f32[512]{0:T(512)S(1)} all-reduce(f32[512]{0:T(512)S(1)} %multiply_reduce_fusion.1), channel_id=1, replica_groups=mesh['patch'=128,'mp'=4] {'mp'}, use_global_device_ids=true, to_apply=%region_5.6 | all-reduce | flops 512 | bytes 4096 | tf_op jit(solution)/shard_map/psum | solution.py:71
  130.6 1.8 multiply_convert_fusion
  132.3 0.0 all-gather.2.cloned.1.call-update
  132.4 0.0 copy-start.4
  132.4 0.0 reduce-scatter.5.cloned.1.call-start
  132.4 32.9 %all-gather.2.cloned.1.call-done = bf16[512,1024]{1,0:T(8,128)(2,1)} async-done(((bf16[512,256]{1,0:T(8,128)(2,1)}), bf16[512,1024]{1,0:T(8,128)(2,1)}) %all-gather.2.cloned.1.call-update) | async-done | bytes 1048592 | tf_op jit(solution)/shard_map/all_gather | solution.py:74
  165.3 3.6 %convolution_convert_fusion.1 = bf16[512,1024]{1,0:T(8,128)(2,1)} fusion(bf16[512,1024]{1,0:T(8,128)(2,1)S(1)} %copy-done, bf16[512,1024]{1,0:T(8,128)(2,1)} %all-gather.2.cloned.1.call-done, bf16[1024,512]{1,0:T(8,128)(2,1)S(1)} %copy-done.7), kind=kOutput, calls=%fused_computation.19 | convolution fusion | flops 1076625408 | bytes 4194304 | tf_op jit(solution)/shard_map/dot_general | solution.py:78
  168.9 0.0 reduce-scatter.5.cloned.1.call-update
  168.9 32.6 %reduce-scatter.5.cloned.1.call-done = bf16[512,256]{1,0:T(8,128)(2,1)} async-done(((bf16[512,1024]{1,0:T(8,128)(2,1)}), bf16[512,256]{1,0:T(8,128)(2,1)}) %reduce-scatter.5.cloned.1.call-update) | async-done | bytes 262160 | tf_op jit(solution)/shard_map/reduce_scatter | solution.py:79
  201.5 1.8 add_convert_fusion
  (15 shorter events, 0.0 us)
Async XLA Ops:
  6.5 158.8 %copy-start = (bf16[512,1024]{1,0:T(8,128)(2,1)S(1)}, bf16[512,1024]{1,0:T(8,128)(2,1)}, u32[]{:S(2)}) copy-start(bf16[512,1024]{1,0:T(8,128)(2,1)} %param.14) | copy-start | bytes 3145732
  6.5 23.1 %copy-start.2 = (bf16[512,1024]{1,0:T(8,128)(2,1)S(1)}, bf16[512,1024]{1,0:T(8,128)(2,1)}, u32[]{:S(2)}) copy-start(bf16[512,1024]{1,0:T(8,128)(2,1)} %param.8) | copy-start | bytes 3145732
  6.5 23.1 %copy-start.8 = (f32[1024]{0:T(1024)S(1)}, f32[1024]{0:T(1024)}, u32[]{:S(2)}) copy-start(f32[1024]{0:T(1024)} %param.9) | copy-start | bytes 12292
  6.5 114.5 %reduce-scatter.3.cloned.1.call-start = ((), (), s32[]{:S(2)}) async-start(), calls=%async_computation.2 | async-start | bytes 1310720 | tf_op jit(solution)/shard_map/reduce_scatter | solution.py:62
  6.5 23.1 %copy-start.6 = (bf16[3,1024,256]{2,1,0:T(8,128)(2,1)S(1)}, bf16[3,1024,256]{2,1,0:T(8,128)(2,1)}, u32[]{:S(2)}) copy-start(bf16[3,1024,256]{2,1,0:T(8,128)(2,1)} %param.10) | copy-start | bytes 4718596
  10.1 24.5 %collective-permute-start.4 = (bf16[4,128,256]{2,1,0:T(8,128)(2,1)S(1)}, bf16[4,128,256]{2,1,0:T(8,128)(2,1)}, u32[]{:S(2)}, u32[]{:S(2)}) collective-permute-start(bf16[4,128,256]{2,1,0:T(8,128)(2,1)S(1)} %bitcast.30), channel_id=1, source_target_pairs={{0,8},{4,12},{8,16},{12,20},{16,24},{20,28},{24,32},{28,36},{32,40... | collective-permute-start | bytes 786440 | tf_op jit(solution)/shard_map/ppermute | solution.py:15
  13.6 24.6 %collective-permute-start.5 = (bf16[4,128,256]{2,1,0:T(8,128)(2,1)S(1)}, bf16[4,128,256]{2,1,0:T(8,128)(2,1)}, u32[]{:S(2)}, u32[]{:S(2)}) collective-permute-start(bf16[4,128,256]{2,1,0:T(8,128)(2,1)S(1)} %bitcast.31), channel_id=1, source_target_pairs={{0,4},{4,8},{8,12},{12,16},{16,20},{20,24},{24,28},{28,32},{32,36}... | collective-permute-start | bytes 786440 | tf_op jit(solution)/shard_map/ppermute | solution.py:15
  15.5 28.7 %collective-permute-start.6 = (bf16[4,128,256]{2,1,0:T(8,128)(2,1)S(1)}, bf16[4,128,256]{2,1,0:T(8,128)(2,1)S(1)}, u32[]{:S(2)}, u32[]{:S(2)}) collective-permute-start(bf16[4,128,256]{2,1,0:T(8,128)(2,1)S(1)} %bitcast.32), channel_id=1, source_target_pairs={{0,508},{4,0},{8,4},{12,8},{16,12},{20,16},{24,20},{28,24},{32,28}... | collective-permute-start | bytes 786440 | tf_op jit(solution)/shard_map/ppermute | solution.py:15
  19.2 33.3 %collective-permute-start.7 = (bf16[4,128,256]{2,1,0:T(8,128)(2,1)S(1)}, bf16[4,128,256]{2,1,0:T(8,128)(2,1)S(1)}, u32[]{:S(2)}, u32[]{:S(2)}) collective-permute-start(bf16[4,128,256]{2,1,0:T(8,128)(2,1)S(1)} %bitcast.33), channel_id=1, source_target_pairs={{0,504},{4,508},{8,0},{12,4},{16,8},{20,12},{24,16},{28,20},{32,24... | collective-permute-start | bytes 786440 | tf_op jit(solution)/shard_map/ppermute | solution.py:15
  30.1 35.1 %collective-permute-start = (bf16[4,128,256]{2,1,0:T(8,128)(2,1)S(1)}, bf16[4,128,256]{2,1,0:T(8,128)(2,1)}, u32[]{:S(2)}, u32[]{:S(2)}) collective-permute-start(bf16[4,128,256]{2,1,0:T(8,128)(2,1)S(1)} %bitcast.25), channel_id=1, source_target_pairs={{0,8},{4,12},{8,16},{12,20},{16,24},{20,28},{24,32},{28,36},{32,40... | collective-permute-start | bytes 786440 | tf_op jit(solution)/shard_map/ppermute | solution.py:15
  34.6 32.4 %collective-permute-start.1 = (bf16[4,128,256]{2,1,0:T(8,128)(2,1)S(1)}, bf16[4,128,256]{2,1,0:T(8,128)(2,1)}, u32[]{:S(2)}, u32[]{:S(2)}) collective-permute-start(bf16[4,128,256]{2,1,0:T(8,128)(2,1)S(1)} %bitcast.26), channel_id=1, source_target_pairs={{0,4},{4,8},{8,12},{12,16},{16,20},{20,24},{24,28},{28,32},{32,36}... | collective-permute-start | bytes 786440 | tf_op jit(solution)/shard_map/ppermute | solution.py:15
  38.2 31.2 %collective-permute-start.2 = (bf16[4,128,256]{2,1,0:T(8,128)(2,1)S(1)}, bf16[4,128,256]{2,1,0:T(8,128)(2,1)}, u32[]{:S(2)}, u32[]{:S(2)}) collective-permute-start(bf16[4,128,256]{2,1,0:T(8,128)(2,1)S(1)} %bitcast.27), channel_id=1, source_target_pairs={{0,508},{4,0},{8,4},{12,8},{16,12},{20,16},{24,20},{28,24},{32,28}... | collective-permute-start | bytes 786440 | tf_op jit(solution)/shard_map/ppermute | solution.py:15
  44.2 26.9 %collective-permute-start.3 = (bf16[4,128,256]{2,1,0:T(8,128)(2,1)S(1)}, bf16[4,128,256]{2,1,0:T(8,128)(2,1)}, u32[]{:S(2)}, u32[]{:S(2)}) collective-permute-start(bf16[4,128,256]{2,1,0:T(8,128)(2,1)S(1)} %bitcast.28), channel_id=1, source_target_pairs={{0,504},{4,508},{8,0},{12,4},{16,8},{20,12},{24,16},{28,20},{32,24... | collective-permute-start | bytes 786440 | tf_op jit(solution)/shard_map/ppermute | solution.py:15
  62.0 3.2 %copy-start.1 = (f32[4,4,128,1024]{3,2,1,0:T(8,128)}, f32[4,4,128,1024]{3,2,1,0:T(8,128)S(1)}, u32[]{:S(2)}) copy-start(f32[4,4,128,1024]{3,2,1,0:T(8,128)S(1)} %fusion.4) | copy-start | bytes 25165828
  78.0 12.4 %copy-start.5 = (bf16[256,1024]{1,0:T(8,128)(2,1)S(1)}, bf16[256,1024]{1,0:T(8,128)(2,1)}, u32[]{:S(2)}) copy-start(bf16[256,1024]{1,0:T(8,128)(2,1)} %param.11) | copy-start | bytes 1572868
  90.1 30.9 %copy-start.3 = (bf16[512,1024]{1,0:T(8,128)(2,1)S(1)}, bf16[512,1024]{1,0:T(8,128)(2,1)}, u32[]{:S(2)}) copy-start(bf16[512,1024]{1,0:T(8,128)(2,1)} %param.8) | copy-start | bytes 3145732
  91.8 73.5 %copy-start.7 = (bf16[1024,512]{1,0:T(8,128)(2,1)S(1)}, bf16[1024,512]{1,0:T(8,128)(2,1)}, u32[]{:S(2)}) copy-start(bf16[1024,512]{1,0:T(8,128)(2,1)} %param.13) | copy-start | bytes 3145732
  91.8 73.5 %all-gather.2.cloned.1.call-start = ((), (), s32[]{:S(2)}) async-start(), calls=%async_computation.3 | async-start | bytes 1310720 | tf_op jit(solution)/shard_map/all_gather | solution.py:74
  132.4 69.1 %copy-start.4 = (bf16[512,256]{1,0:T(8,128)(2,1)S(1)}, bf16[512,256]{1,0:T(8,128)(2,1)}, u32[]{:S(2)}) copy-start(bf16[512,256]{1,0:T(8,128)(2,1)} %reduce-scatter.3.cloned.1.call-done) | copy-start | bytes 786436
  132.4 69.1 %reduce-scatter.5.cloned.1.call-start = ((), (), s32[]{:S(2)}) async-start(), calls=%async_computation.4 | async-start | bytes 1310720 | tf_op jit(solution)/shard_map/reduce_scatter | solution.py:79
Sparse Core Ops, SparseCore 0:
  92.0 29.0 reduce-scatter.2
  132.5 32.8 all-gather.1
  169.1 32.3 reduce-scatter.4
where the time goes:
time: 211 us; the launch traced here: 210 us
  waiting for transfers between devices  93.9 us (45%)
  starting transfers between devices  34.6 us (16%)
  local copies, waits for them, and re-layouts  26.8 us (13%)
  matrix products  23.6 us (11%)
  between operations  13.3 us (6%)
  other arithmetic  9.3 us (4%)
  blocking collectives  8.37 us (4%)
    ppermute x8, starting transfers between devices, from_behind(): lax.ppermute(array, axis, [(i, (i + by) % length) for i in range(length)])  34.5 us
    all_gather x1, waiting for transfers between devices, per_device(): normed2 = lax.all_gather(normed_cols, 'mp', axis=1, tiled=True)  32.9 us
    reduce_scatter x1, waiting for transfers between devices, per_device(): lax.psum_scatter(down_term.astype(jnp.bfloat16), 'mp', scatter_dimension=...  32.6 us
    reduce_scatter x1, waiting for transfers between devices, per_device(): lax.psum_scatter(partial_value.astype(jnp.bfloat16), 'mp', scatter_dimens...  28.3 us
    dot_general x1, matrix products, per_device(): jnp.einsum('phqk,pkhd->pqhd', probs, vals_nb, preferred_element_type=jnp....  12.1 us
    unnamed x26, local copies, waits for them, and re-layouts  11.6 us
    psum x1, blocking collectives, per_device(): square_sum = lax.psum(jnp.sum(residual_cols * residual_cols, axis=1), 'mp')  8.37 us
  transfers between devices with their start and end apart: 11, of which 3 were waited for; matrix products, arithmetic and copies ran while one was open for 12% of the time, Pallas kernels for 0%

commit v1 on v0

--- a/solution.py
+++ b/solution.py
@@ -8,6 +8,11 @@
 PN = 128
 K_NB = 8
 REACH = 2
+
+
+def gather_from_all(value, axis, dim):
+    copies = jnp.concatenate([value] * lax.axis_size(axis), axis=dim)
+    return lax.all_to_all(copies, axis, dim, dim, tiled=True)
 
 
 def from_behind(array, axis, by):
@@ -71,7 +76,7 @@
     square_sum = lax.psum(jnp.sum(residual_cols * residual_cols, axis=1), "mp")
     inverse_rms = lax.rsqrt(square_sum / D + 1e-05)
     normed_cols = (residual_cols * inverse_rms[:, None] * gain_cols).astype(jnp.bfloat16)
-    normed2 = lax.all_gather(normed_cols, "mp", axis=1, tiled=True)
+    normed2 = gather_from_all(normed_cols, "mp", 1)
     hidden = jax.nn.gelu(
         jnp.dot(normed2, w_up, preferred_element_type=jnp.float32), approximate=True
     ).astype(jnp.bfloat16)

time: 211 us -> 192 us (0.910)
  waiting for transfers between devices: 93.9 us -> 59.5 us
  blocking collectives: 8.37 us -> 23 us
    all_gather x1 -> x0, waiting for transfers between devices: 32.9 us -> none  [per_device(): normed2 = lax.all_gather(normed_cols, 'mp', axis=1, tiled=True)]
    all_to_all x0 -> x1, blocking collectives: none -> 14.7 us  [gather_from_all(): return lax.all_to_all(copies, axis, dim, dim, tiled=True)]
    unnamed x26 -> x24, local copies, waits for them, and re-layouts: 11.6 us -> 11.6 us
  transfers between devices with their start and end apart: 11 -> 10, of which waited for: 3 -> 2; matrix products, arithmetic and copies ran while one was open for 12% -> 14% of each run, Pallas kernels for 0% -> 0%
where the time goes in v1:
time: 192 us; the launch traced here: 191 us
  waiting for transfers between devices  59.5 us (31%)
  starting transfers between devices  34.5 us (18%)
  local copies, waits for them, and re-layouts  28.2 us (15%)
  matrix products  24 us (12%)
  blocking collectives  23 us (12%)
  between operations  13.6 us (7%)
  other arithmetic  8.66 us (5%)
    ppermute x8, starting transfers between devices, from_behind(): lax.ppermute(array, axis, [(i, (i + by) % length) for i in range(length)])  34.5 us
    reduce_scatter x1, waiting for transfers between devices, per_device(): lax.psum_scatter(down_term.astype(jnp.bfloat16), 'mp', scatter_dimension=...  31.1 us
    reduce_scatter x1, waiting for transfers between devices, per_device(): lax.psum_scatter(partial_value.astype(jnp.bfloat16), 'mp', scatter_dimens...  28.4 us
    all_to_all x1, blocking collectives, gather_from_all(): return lax.all_to_all(copies, axis, dim, dim, tiled=True)  14.7 us
    dot_general x1, matrix products, per_device(): jnp.einsum('phqk,pkhd->pqhd', probs, vals_nb, preferred_element_type=jnp....  12.1 us
    unnamed x24, local copies, waits for them, and re-layouts  11.6 us
    psum x1, blocking collectives, per_device(): square_sum = lax.psum(jnp.sum(residual_cols * residual_cols, axis=1), 'mp')  8.31 us
    dot_general x1, matrix products, per_device(): down_term = jnp.dot(hidden, w_down, preferred_element_type=jnp.float32)  3.97 us
  transfers between devices with their start and end apart: 10, of which 2 were waited for; matrix products, arithmetic and copies ran while one was open for 14% of the time, Pallas kernels for 0%

profile of v1, /device:TPU:8, one launch (start us, length us, event | category | flops | bytes accessed | tf_op | source)
XLA Modules:
  0.0 191.4 jit_solution(1558125088424479848)
XLA Ops:
  6.5 0.0 copy-start.6
  6.6 1.7 fusion.9
  8.2 1.9 convolution_convert_fusion.2
  10.1 3.5 %collective-permute-start.4 = (bf16[4,128,256]{2,1,0:T(8,128)(2,1)S(1)}, bf16[4,128,256]{2,1,0:T(8,128)(2,1)}, u32[]{:S(2)}, u32[]{:S(2)}) collective-permute-start(bf16[4,128,256]{2,1,0:T(8,128)(2,1)S(1)} %bitcast.38), channel_id=1, source_target_pairs={{0,8},{4,12},{8,16},{12,20},{16,24},{20,28},{24,32},{28,36},{32,40... | collective-permute-start | bytes 786440 | tf_op jit(solution)/shard_map/ppermute | solution.py:20
  13.6 1.9 %collective-permute-start.5 = (bf16[4,128,256]{2,1,0:T(8,128)(2,1)S(1)}, bf16[4,128,256]{2,1,0:T(8,128)(2,1)}, u32[]{:S(2)}, u32[]{:S(2)}) collective-permute-start(bf16[4,128,256]{2,1,0:T(8,128)(2,1)S(1)} %bitcast.39), channel_id=1, source_target_pairs={{0,4},{4,8},{8,12},{12,16},{16,20},{20,24},{24,28},{28,32},{32,36}... | collective-permute-start | bytes 786440 | tf_op jit(solution)/shard_map/ppermute | solution.py:20
  15.5 3.6 %collective-permute-start.6 = (bf16[4,128,256]{2,1,0:T(8,128)(2,1)S(1)}, bf16[4,128,256]{2,1,0:T(8,128)(2,1)S(1)}, u32[]{:S(2)}, u32[]{:S(2)}) collective-permute-start(bf16[4,128,256]{2,1,0:T(8,128)(2,1)S(1)} %bitcast.40), channel_id=1, source_target_pairs={{0,508},{4,0},{8,4},{12,8},{16,12},{20,16},{24,20},{28,24},{32,28}... | collective-permute-start | bytes 786440 | tf_op jit(solution)/shard_map/ppermute | solution.py:20
  19.2 10.4 %collective-permute-start.7 = (bf16[4,128,256]{2,1,0:T(8,128)(2,1)S(1)}, bf16[4,128,256]{2,1,0:T(8,128)(2,1)S(1)}, u32[]{:S(2)}, u32[]{:S(2)}) collective-permute-start(bf16[4,128,256]{2,1,0:T(8,128)(2,1)S(1)} %bitcast.41), channel_id=1, source_target_pairs={{0,504},{4,508},{8,0},{12,4},{16,8},{20,12},{24,16},{28,20},{32,24... | collective-permute-start | bytes 786440 | tf_op jit(solution)/shard_map/ppermute | solution.py:20
  29.6 0.0 copy-done.2
  29.6 0.0 copy-done.7
  29.6 0.0 copy-done.6
  29.7 0.5 convolution_convert_fusion.4
  30.1 1.9 %collective-permute-start = (bf16[4,128,256]{2,1,0:T(8,128)(2,1)S(1)}, bf16[4,128,256]{2,1,0:T(8,128)(2,1)}, u32[]{:S(2)}, u32[]{:S(2)}) collective-permute-start(bf16[4,128,256]{2,1,0:T(8,128)(2,1)S(1)} %bitcast.33), channel_id=1, source_target_pairs={{0,8},{4,12},{8,16},{12,20},{16,24},{20,28},{24,32},{28,36},{32,40... | collective-permute-start | bytes 786440 | tf_op jit(solution)/shard_map/ppermute | solution.py:20
  32.1 0.5 convolution_convert_fusion.3
  32.6 0.8 compare_select_fusion
  33.4 0.1 copy.34
  33.5 0.1 reshape.41
  33.5 1.0 reshape.62
  34.6 0.0 collective-permute-done.4
  34.6 1.9 %collective-permute-start.1 = (bf16[4,128,256]{2,1,0:T(8,128)(2,1)S(1)}, bf16[4,128,256]{2,1,0:T(8,128)(2,1)}, u32[]{:S(2)}, u32[]{:S(2)}) collective-permute-start(bf16[4,128,256]{2,1,0:T(8,128)(2,1)S(1)} %bitcast.34), channel_id=1, source_target_pairs={{0,4},{4,8},{8,12},{12,16},{16,20},{20,24},{24,28},{28,32},{32,36}... | collective-permute-start | bytes 786440 | tf_op jit(solution)/shard_map/ppermute | solution.py:20
  36.5 1.7 constant_dynamic-update-slice_fusion.9
  38.2 0.0 collective-permute-done.5
  38.2 3.6 %collective-permute-start.2 = (bf16[4,128,256]{2,1,0:T(8,128)(2,1)S(1)}, bf16[4,128,256]{2,1,0:T(8,128)(2,1)}, u32[]{:S(2)}, u32[]{:S(2)}) collective-permute-start(bf16[4,128,256]{2,1,0:T(8,128)(2,1)S(1)} %bitcast.35), channel_id=1, source_target_pairs={{0,508},{4,0},{8,4},{12,8},{16,12},{20,16},{24,20},{28,24},{32,28}... | collective-permute-start | bytes 786440 | tf_op jit(solution)/shard_map/ppermute | solution.py:20
  41.8 1.7 constant_dynamic-update-slice_fusion.8
  43.5 0.7 constant_dynamic-update-slice_fusion.7
  44.2 0.0 collective-permute-done.6
  44.2 7.5 %collective-permute-start.3 = (bf16[4,128,256]{2,1,0:T(8,128)(2,1)S(1)}, bf16[4,128,256]{2,1,0:T(8,128)(2,1)}, u32[]{:S(2)}, u32[]{:S(2)}) collective-permute-start(bf16[4,128,256]{2,1,0:T(8,128)(2,1)S(1)} %bitcast.36), channel_id=1, source_target_pairs={{0,504},{4,508},{8,0},{12,4},{16,8},{20,12},{24,16},{28,20},{32,24... | collective-permute-start | bytes 786440 | tf_op jit(solution)/shard_map/ppermute | solution.py:20
  51.7 0.7 constant_dynamic-update-slice_fusion.6
  52.5 0.0 collective-permute-done.7
  52.5 0.7 constant_dynamic-update-slice_fusion.5
  53.2 2.0 %gather_fusion.1 = bf16[32,128,256]{2,1,0:T(8,128)(2,1)S(1)} fusion(bf16[20,128,256]{2,1,0:T(8,128)(2,1)} %constant_dynamic-update-slice_fusion.5, s32[1024]{0:T(1024)S(1)} %pad_clamp_fusion), kind=kCustom, calls=%fused_computation.1 | custom fusion | bytes 4194432 | tf_op jit(solution)/shard_map/gather | solution.py:57
  55.2 3.3 %reshape.63 = bf16[4,1024,4,64]{3,2,1,0:T(4,128)(2,1)} reshape(bf16[32,128,256]{2,1,0:T(8,128)(2,1)S(1)} %gather_fusion.1) | data formatting | bytes 4194304 | tf_op jit(solution)/shard_map/reshape | solution.py:57
  58.5 3.6 %fusion.4 = f32[4,4,128,1024]{3,2,1,0:T(8,128)S(1)} fusion(bf16[4,1024,4,64]{3,2,1,0:T(4,128)(2,1)} %reshape.63, bf16[4,128,4,64]{3,2,1,0:T(4,128)(2,1)} %reshape.62), kind=kOutput, calls=%fused_computation.7 | convolution fusion | flops 268435456 | bytes 10747904 | tf_op jit(solution)/shard_map/pqhd,pkhd->phqk/dot_general | solution.py:60
  62.1 2.2 %fusion.62 = f32[4,4,128]{2,1,0:T(4,128)S(1)} fusion(f32[4,4,128,1024]{3,2,1,0:T(8,128)S(1)} %fusion.4), kind=kOutput, calls=%fused_computation.89 | output fusion | flops 8389631 | bytes 8396800 | tf_op jit(solution)/shard_map/sub | solution.py:63
  64.3 1.0 copy-done.1
  65.3 0.0 collective-permute-done
  65.3 1.7 constant_dynamic-update-slice_fusion.4
  67.0 0.0 collective-permute-done.1
  67.0 1.7 constant_dynamic-update-slice_fusion.3
  68.7 0.7 constant_dynamic-update-slice_fusion.2
  69.4 0.0 collective-permute-done.2
  69.4 1.7 constant_dynamic-update-slice_fusion.1
  71.1 0.0 collective-permute-done.3
  71.1 1.7 constant_dynamic-update-slice_fusion
  72.8 2.0 %gather_fusion = bf16[32,128,256]{2,1,0:T(8,128)(2,1)S(1)} fusion(bf16[20,128,256]{2,1,0:T(8,128)(2,1)} %constant_dynamic-update-slice_fusion, s32[1024]{0:T(1024)S(1)} %pad_clamp_fusion), kind=kCustom, calls=%fused_computation | custom fusion | bytes 4194432 | tf_op jit(solution)/shard_map/gather | solution.py:58
  74.8 3.3 %reshape.61 = bf16[4,1024,4,64]{3,2,1,0:T(4,128)(2,1)} reshape(bf16[32,128,256]{2,1,0:T(8,128)(2,1)S(1)} %gather_fusion) | data formatting | bytes 4194304 | tf_op jit(solution)/shard_map/reshape | solution.py:58
  78.1 12.1 %fusion.15 = bf16[4,128,4,64]{1,3,2,0:T(8,128)(2,1)S(1)} fusion(f32[4,4,128]{2,1,0:T(4,128)S(1)} %fusion.62, bf16[4,1024,4,64]{3,2,1,0:T(4,128)(2,1)} %reshape.61, f32[4,4,128,1024]{3,2,1,0:T(8,128)} %copy-done.1), kind=kOutput, calls=%fused_computation.24 | convolution fusion | flops 279055360 | bytes 10756096 | tf_op jit(solution)/shard_map/phqk,pkhd->pqhd/dot_general | solution.py:64
  90.2 0.0 copy-start.3
  90.2 0.2 copy.41
  90.4 1.5 convolution_convert_fusion
  91.9 0.0 reduce-scatter.3.cloned.1.call-update
  91.9 0.0 reduce-scatter.5.cloned.1.call-start
  92.0 0.8 dynamic_slice.11
  92.7 28.4 %reduce-scatter.3.cloned.1.call-done = bf16[512,256]{1,0:T(8,128)(2,1)} async-done(((bf16[512,1024]{1,0:T(8,128)(2,1)}), bf16[512,256]{1,0:T(8,128)(2,1)}) %reduce-scatter.3.cloned.1.call-update) | async-done | bytes 262160 | tf_op jit(solution)/shard_map/reduce_scatter | solution.py:67
  121.1 1.1 multiply_reduce_fusion.1
  122.2 8.3 %psum.7 = f32[512]{0:T(512)S(1)} all-reduce(f32[512]{0:T(512)S(1)} %multiply_reduce_fusion.1), channel_id=1, replica_groups=mesh['patch'=128,'mp'=4] {'mp'}, use_global_device_ids=true, to_apply=%region_5.6 | all-reduce | flops 512 | bytes 4096 | tf_op jit(solution)/shard_map/psum | solution.py:76
  130.5 1.1 multiply_convert_fusion
  131.6 0.1 pad_maximum_fusion
  131.7 0.1 copy.67
  131.8 14.7 %all_to_all.12 = bf16[512,4,256]{2,0,1:T(8,128)(2,1)S(1)} all-to-all(bf16[512,4,256]{2,0,1:T(8,128)(2,1)S(1)} %bitcast.30), channel_id=1, replica_groups=mesh['patch'=128,'mp'=4] {'mp'}, dimensions={1} | all-to-all | bytes 2097152 | tf_op jit(solution)/shard_map/all_to_all | solution.py:15
  146.5 1.3 copy.43
  147.8 4.0 %convolution_convert_fusion.1 = bf16[512,1024]{1,0:T(8,128)(2,1)} fusion(bf16[512,1024]{1,0:T(8,128)(2,1)S(1)} %copy-done, bf16[512,1024]{0,1:T(8,128)(2,1)} %bitcast.32, bf16[1024,512]{1,0:T(8,128)(2,1)} %param.13), kind=kOutput, calls=%fused_computation.19 | convolution fusion | flops 1076625408 | bytes 4194304 | tf_op jit(solution)/shard_map/dot_general | solution.py:83
  151.8 0.0 reduce-scatter.5.cloned.1.call-update
  151.8 31.1 %reduce-scatter.5.cloned.1.call-done = bf16[512,256]{1,0:T(8,128)(2,1)} async-done(((bf16[512,1024]{1,0:T(8,128)(2,1)}), bf16[512,256]{1,0:T(8,128)(2,1)}) %reduce-scatter.5.cloned.1.call-update) | async-done | bytes 262160 | tf_op jit(solution)/shard_map/reduce_scatter | solution.py:84
  182.9 1.8 add_convert_fusion
  (14 shorter events, 0.0 us)
Async XLA Ops:
  6.5 141.3 %copy-start = (bf16[512,1024]{1,0:T(8,128)(2,1)S(1)}, bf16[512,1024]{1,0:T(8,128)(2,1)}, u32[]{:S(2)}) copy-start(bf16[512,1024]{1,0:T(8,128)(2,1)} %param.14) | copy-start | bytes 3145732
  6.5 23.1 %copy-start.2 = (bf16[512,1024]{1,0:T(8,128)(2,1)S(1)}, bf16[512,1024]{1,0:T(8,128)(2,1)}, u32[]{:S(2)}) copy-start(bf16[512,1024]{1,0:T(8,128)(2,1)} %param.8) | copy-start | bytes 3145732
  6.5 23.1 %copy-start.7 = (f32[1024]{0:T(1024)S(1)}, f32[1024]{0:T(1024)}, u32[]{:S(2)}) copy-start(f32[1024]{0:T(1024)} %param.9) | copy-start | bytes 12292
  6.5 114.6 %reduce-scatter.3.cloned.1.call-start = ((), (), s32[]{:S(2)}) async-start(), calls=%async_computation.3 | async-start | bytes 1310720 | tf_op jit(solution)/shard_map/reduce_scatter | solution.py:67
  6.5 23.1 %copy-start.6 = (bf16[3,1024,256]{2,1,0:T(8,128)(2,1)S(1)}, bf16[3,1024,256]{2,1,0:T(8,128)(2,1)}, u32[]{:S(2)}) copy-start(bf16[3,1024,256]{2,1,0:T(8,128)(2,1)} %param.10) | copy-start | bytes 4718596
  10.1 24.5 %collective-permute-start.4 = (bf16[4,128,256]{2,1,0:T(8,128)(2,1)S(1)}, bf16[4,128,256]{2,1,0:T(8,128)(2,1)}, u32[]{:S(2)}, u32[]{:S(2)}) collective-permute-start(bf16[4,128,256]{2,1,0:T(8,128)(2,1)S(1)} %bitcast.38), channel_id=1, source_target_pairs={{0,8},{4,12},{8,16},{12,20},{16,24},{20,28},{24,32},{28,36},{32,40... | collective-permute-start | bytes 786440 | tf_op jit(solution)/shard_map/ppermute | solution.py:20
  13.6 24.6 %collective-permute-start.5 = (bf16[4,128,256]{2,1,0:T(8,128)(2,1)S(1)}, bf16[4,128,256]{2,1,0:T(8,128)(2,1)}, u32[]{:S(2)}, u32[]{:S(2)}) collective-permute-start(bf16[4,128,256]{2,1,0:T(8,128)(2,1)S(1)} %bitcast.39), channel_id=1, source_target_pairs={{0,4},{4,8},{8,12},{12,16},{16,20},{20,24},{24,28},{28,32},{32,36}... | collective-permute-start | bytes 786440 | tf_op jit(solution)/shard_map/ppermute | solution.py:20
  15.5 28.7 %collective-permute-start.6 = (bf16[4,128,256]{2,1,0:T(8,128)(2,1)S(1)}, bf16[4,128,256]{2,1,0:T(8,128)(2,1)S(1)}, u32[]{:S(2)}, u32[]{:S(2)}) collective-permute-start(bf16[4,128,256]{2,1,0:T(8,128)(2,1)S(1)} %bitcast.40), channel_id=1, source_target_pairs={{0,508},{4,0},{8,4},{12,8},{16,12},{20,16},{24,20},{28,24},{32,28}... | collective-permute-start | bytes 786440 | tf_op jit(solution)/shard_map/ppermute | solution.py:20
  19.2 33.3 %collective-permute-start.7 = (bf16[4,128,256]{2,1,0:T(8,128)(2,1)S(1)}, bf16[4,128,256]{2,1,0:T(8,128)(2,1)S(1)}, u32[]{:S(2)}, u32[]{:S(2)}) collective-permute-start(bf16[4,128,256]{2,1,0:T(8,128)(2,1)S(1)} %bitcast.41), channel_id=1, source_target_pairs={{0,504},{4,508},{8,0},{12,4},{16,8},{20,12},{24,16},{28,20},{32,24... | collective-permute-start | bytes 786440 | tf_op jit(solution)/shard_map/ppermute | solution.py:20
  30.1 35.2 %collective-permute-start = (bf16[4,128,256]{2,1,0:T(8,128)(2,1)S(1)}, bf16[4,128,256]{2,1,0:T(8,128)(2,1)}, u32[]{:S(2)}, u32[]{:S(2)}) collective-permute-start(bf16[4,128,256]{2,1,0:T(8,128)(2,1)S(1)} %bitcast.33), channel_id=1, source_target_pairs={{0,8},{4,12},{8,16},{12,20},{16,24},{20,28},{24,32},{28,36},{32,40... | collective-permute-start | bytes 786440 | tf_op jit(solution)/shard_map/ppermute | solution.py:20
  34.6 32.4 %collective-permute-start.1 = (bf16[4,128,256]{2,1,0:T(8,128)(2,1)S(1)}, bf16[4,128,256]{2,1,0:T(8,128)(2,1)}, u32[]{:S(2)}, u32[]{:S(2)}) collective-permute-start(bf16[4,128,256]{2,1,0:T(8,128)(2,1)S(1)} %bitcast.34), channel_id=1, source_target_pairs={{0,4},{4,8},{8,12},{12,16},{16,20},{20,24},{24,28},{28,32},{32,36}... | collective-permute-start | bytes 786440 | tf_op jit(solution)/shard_map/ppermute | solution.py:20
  38.2 31.2 %collective-permute-start.2 = (bf16[4,128,256]{2,1,0:T(8,128)(2,1)S(1)}, bf16[4,128,256]{2,1,0:T(8,128)(2,1)}, u32[]{:S(2)}, u32[]{:S(2)}) collective-permute-start(bf16[4,128,256]{2,1,0:T(8,128)(2,1)S(1)} %bitcast.35), channel_id=1, source_target_pairs={{0,508},{4,0},{8,4},{12,8},{16,12},{20,16},{24,20},{28,24},{32,28}... | collective-permute-start | bytes 786440 | tf_op jit(solution)/shard_map/ppermute | solution.py:20
  44.2 26.9 %collective-permute-start.3 = (bf16[4,128,256]{2,1,0:T(8,128)(2,1)S(1)}, bf16[4,128,256]{2,1,0:T(8,128)(2,1)}, u32[]{:S(2)}, u32[]{:S(2)}) collective-permute-start(bf16[4,128,256]{2,1,0:T(8,128)(2,1)S(1)} %bitcast.36), channel_id=1, source_target_pairs={{0,504},{4,508},{8,0},{12,4},{16,8},{20,12},{24,16},{28,20},{32,24... | collective-permute-start | bytes 786440 | tf_op jit(solution)/shard_map/ppermute | solution.py:20
  62.1 3.2 %copy-start.1 = (f32[4,4,128,1024]{3,2,1,0:T(8,128)}, f32[4,4,128,1024]{3,2,1,0:T(8,128)S(1)}, u32[]{:S(2)}) copy-start(f32[4,4,128,1024]{3,2,1,0:T(8,128)S(1)} %fusion.4) | copy-start | bytes 25165828
  78.1 12.4 %copy-start.5 = (bf16[256,1024]{1,0:T(8,128)(2,1)S(1)}, bf16[256,1024]{1,0:T(8,128)(2,1)}, u32[]{:S(2)}) copy-start(bf16[256,1024]{1,0:T(8,128)(2,1)} %param.11) | copy-start | bytes 1572868
  90.2 30.9 %copy-start.3 = (bf16[512,1024]{1,0:T(8,128)(2,1)S(1)}, bf16[512,1024]{1,0:T(8,128)(2,1)}, u32[]{:S(2)}) copy-start(bf16[512,1024]{1,0:T(8,128)(2,1)} %param.8) | copy-start | bytes 3145732
  91.9 90.9 %reduce-scatter.5.cloned.1.call-start = ((), (), s32[]{:S(2)}) async-start(), calls=%async_computation.4 | async-start | bytes 1310720 | tf_op jit(solution)/shard_map/reduce_scatter | solution.py:84
  147.8 35.1 %copy-start.4 = (bf16[512,256]{1,0:T(8,128)(2,1)S(1)}, bf16[512,256]{1,0:T(8,128)(2,1)}, u32[]{:S(2)}) copy-start(bf16[512,256]{1,0:T(8,128)(2,1)} %reduce-scatter.3.cloned.1.call-done) | copy-start | bytes 786436
Sparse Core Ops, SparseCore 0:
  92.0 29.0 reduce-scatter.2
  151.9 30.8 reduce-scatter.4
